TPU v7x, 512 devices: a whole 4x8x8 slice. The times are simulated.
512 devices in a mesh: row: 32 (over z, x), col: 16 (over y, core).
Axes of the slice: x: 4, y: 8, z: 8, core: 2. Of those that a mesh axis runs over, the one named last changes fastest.
Arguments:
- tokens: bfloat16 [16384, 5376], P('row', 'col'), may hold values from -240 to 240
- gain: float32 [5376], P('col'), may hold values from 0.1 to 1.9
- query_gain: float32 [128], replicated, may hold values from 0.1 to 1.9
- key_gain: float32 [128], replicated, may hold values from 0.1 to 1.9
- w_query: bfloat16 [5376, 4096], P('row', 'col'), may hold values from -0.21808224 to 0.21808224
- w_key: bfloat16 [5376, 2048], P('row', 'col'), may hold values from -0.21808224 to 0.21808224
- w_value: bfloat16 [5376, 2048], P('row', 'col'), may hold values from -0.21808224 to 0.21808224
Outputs:
- attended: bfloat16 [16384, 4096], P('row', 'col')
All inputs are finite; a program needn't handle non-finite values.
Results may differ from a plain program's by a relative error of at most 0.022.
Values may be sent and summed in bfloat16 or wider, within the bound.
No kernel may reach another device: no remote copies, remote signals or barrier semaphores. Data moves between devices by JAX's collectives and lax.ppermute only.
A program may use at most 64 MiB of HBM per device.

v0:
```python
import jax
import jax.numpy as jnp
from jax import lax
from jax.sharding import Mesh, PartitionSpec as P

D = 5376
HD = 128
WINDOW = 1024
EPS = 1e-06
CLIP_FRACTION = 0.25
QUERY_SCALAR = 168.0
ROPE_BASE = 10000.0
ROW = ("rz", "rx")


def shifted(array, axis, by):
    peers = lax.axis_size(axis)
    pairs = [(i, i + by) for i in range(peers) if 0 <= i + by < peers]
    return lax.ppermute(array, axis, pairs)


def ring_gather(parts, axis, dims):
    peers = lax.axis_size(axis)
    right = [(i, (i + 1) % peers) for i in range(peers)]
    left = [(i, (i - 1) % peers) for i in range(peers)]
    held = {0: parts}
    forward = parts
    backward = parts
    for step in range(1, peers // 2 + 1):
        forward = lax.ppermute(forward, axis, right)
        held[peers - step] = forward
        if step < peers - step:
            backward = lax.ppermute(backward, axis, left)
            held[step] = backward
    start = (peers - lax.axis_index(axis)) % peers
    out = []
    for leaf, dim in enumerate(dims):
        stacked = jnp.concatenate([held[k][leaf] for k in range(peers)], axis=dim)
        doubled = jnp.concatenate([stacked, stacked], axis=dim)
        size = parts[leaf].shape[dim]
        out.append(lax.dynamic_slice_in_dim(doubled, start * size, peers * size, dim))
    return tuple(out)


def clip_with(weight, largest):
    bound = CLIP_FRACTION * largest
    return jnp.clip(weight.astype(jnp.float32), -bound, bound).astype(jnp.bfloat16)


def column_max(weight):
    return jnp.max(jnp.abs(weight.astype(jnp.float32)), axis=0)


def head_norm(values, head_gain):
    return values * lax.rsqrt(jnp.mean(values * values, axis=-1, keepdims=True) + EPS) * head_gain


def rotate(values, positions):
    half = values.shape[-1] // 2
    freqs = ROPE_BASE ** (-(jnp.arange(half, dtype=jnp.float32) * 2.0 / values.shape[-1]))
    angles = positions.astype(jnp.float32)[:, None] * freqs[None, :]
    cosine = jnp.cos(angles)[:, None, :]
    sine = jnp.sin(angles)[:, None, :]
    first = values[..., :half]
    second = values[..., half:]
    return jnp.concatenate(
        [first * cosine - second * sine, second * cosine + first * sine], axis=-1
    )


def local(tokens, gain, query_gain, key_gain, w_query, w_key, w_value):
    rows = tokens.shape[0]
    query_cols = w_query.shape[1]
    key_cols = w_key.shape[1]
    stacked = jnp.concatenate([w_query, w_key, w_value], axis=1)
    weight_rows, weight_cols = stacked.shape
    aligned = -(-(weight_rows + 1) // TILE_ROWS) * TILE_ROWS
    local_max = jnp.max(jnp.abs(stacked), axis=0)
    padded = jnp.concatenate(
        [
            stacked,
            local_max[None],
            jnp.zeros((aligned - weight_rows - 1, weight_cols), stacked.dtype),
        ],
        axis=0,
    )
    slabs = lax.all_gather(padded, ROW, axis=0, tiled=True).reshape(-1, aligned, weight_cols)
    largest = jnp.max(slabs[:, weight_rows].astype(jnp.float32), axis=0)

    def clipped_columns(first, last):
        part = slabs[:, :weight_rows, first:last].reshape(-1, last - first)
        return clip_with(part, largest[first:last])

    rows_tokens, piece = tokens.shape
    cores = lax.axis_size("cc")
    high = gain.astype(jnp.bfloat16)
    rest = gain - high.astype(jnp.float32)
    middle = rest.astype(jnp.bfloat16)
    low = (rest - middle.astype(jnp.float32)).astype(jnp.bfloat16)
    filler = jnp.zeros((GAIN_ROWS - 3, piece), jnp.bfloat16)
    packed = jnp.concatenate([tokens, high[None], middle[None], low[None], filler], axis=0)
    (along_y,) = ring_gather((packed,), "cy", (1,))
    (along_all,) = ring_gather((along_y,), "cc", (1,))
    blocks = along_all.shape[1] // (cores * piece)
    split = along_all[rows_tokens : rows_tokens + 3].astype(jnp.float32)
    full_gain = split[0] + (split[1] + split[2])
    widened = along_all[:rows_tokens].astype(jnp.float32)
    squares = jnp.sum(widened * widened, axis=1)
    inverse = lax.rsqrt(squares / D + EPS)[:, None]
    whole = (widened * inverse * full_gain[None, :]).astype(jnp.bfloat16)

    def ordered(first, last):
        part = clipped_columns(first, last)
        return (
            part.reshape(blocks, cores, piece, last - first)
            .transpose(1, 0, 2, 3)
            .reshape(part.shape)
        )

    kv_part = jnp.dot(whole, ordered(query_cols, weight_cols), preferred_element_type=jnp.float32)
    keys = kv_part[:, :key_cols]
    values = kv_part[:, key_cols:]
    query = jnp.dot(whole, ordered(0, query_cols), preferred_element_type=jnp.float32)
    heads_local = query_cols // HD
    kv_local = key_cols // HD
    group = heads_local // kv_local
    positions = lax.axis_index(ROW) * rows + jnp.arange(rows, dtype=jnp.int32)
    query = rotate(head_norm(query.reshape(rows, heads_local, HD), query_gain), positions).astype(
        jnp.bfloat16
    )
    keys = rotate(head_norm(keys.reshape(rows, kv_local, HD), key_gain), positions).astype(
        jnp.bfloat16
    )
    values = values.reshape(rows, kv_local, HD).astype(jnp.bfloat16)
    blocks_back = WINDOW // rows
    both = jnp.concatenate([keys, values], axis=1)
    earlier = [shifted(both, ROW, offset) for offset in range(blocks_back, 0, -1)]
    joined = jnp.concatenate(earlier + [both], axis=0)
    all_keys = joined[:, :kv_local]
    all_values = joined[:, kv_local:]
    key_pos = (
        positions[0] - blocks_back * rows + jnp.arange((blocks_back + 1) * rows, dtype=jnp.int32)
    )
    grouped = query.reshape(rows, kv_local, group, HD)
    scores = jnp.einsum(
        "tkgd,skd->kgts", grouped, all_keys, preferred_element_type=jnp.float32
    ) * QUERY_SCALAR ** (-0.5)
    distance = positions[:, None] - key_pos[None, :]
    allowed = (distance >= 0) & (distance < WINDOW) & (key_pos[None, :] >= 0)
    expo = jnp.where(allowed, jnp.exp(scores), 0.0)
    total = jnp.sum(expo, axis=-1, keepdims=True)
    probs = (expo / total).astype(jnp.bfloat16)
    output = jnp.einsum("kgts,skd->tkgd", probs, all_values, preferred_element_type=jnp.float32)
    return output.reshape(rows, query_cols).astype(jnp.bfloat16)


CORES_PER_CHIP = 2
GAIN_ROWS = 8
TILE_ROWS = 16


def solution(mesh):
    rows, cols = (mesh.shape["row"], mesh.shape["col"])
    minor = len({tuple(getattr(d, "coords", (0,)))[0] for d in mesh.devices[:, 0].flat})
    if rows % minor:
        minor = 1
    split = Mesh(
        mesh.devices.reshape(rows // minor, minor, cols // CORES_PER_CHIP, CORES_PER_CHIP),
        ("rz", "rx", "cy", "cc"),
    )
    col = ("cy", "cc")
    placed = (P(ROW, col), P(col), P(), P(), P(ROW, col), P(ROW, col), P(ROW, col))
    return jax.shard_map(local, mesh=split, in_specs=placed, out_specs=P(ROW, col), check_vma=False)
```

profile of v0, /device:TPU:8, one launch (start us, length us, event | category | flops | bytes accessed | tf_op | source)
XLA Modules:
  0.0 144.5 jit_solution(14223948098695784840)
XLA Ops:
  12.2 3.5 %collective-permute-start.3 = (bf16[520,336]{1,0:T(8,128)(2,1)S(1)}, bf16[520,336]{1,0:T(8,128)(2,1)S(1)}, u32[]{:S(2)}, u32[]{:S(2)}) collective-permute-start(bf16[520,336]{1,0:T(8,128)(2,1)S(1)} %concatenate.43), channel_id=1, source_target_pairs={{0,2},{2,4},{4,6},{6,8},{8,10},{10,12},{12,14},{14,0},{1,3},{3,5},... | collective-permute-start | bytes 1048328 | tf_op jit(solution)/shard_map/ppermute | solution.py:30
  15.7 6.2 %collective-permute-start = (bf16[520,336]{1,0:T(8,128)(2,1)S(1)}, bf16[520,336]{1,0:T(8,128)(2,1)S(1)}, u32[]{:S(2)}, u32[]{:S(2)}) collective-permute-start(bf16[520,336]{1,0:T(8,128)(2,1)S(1)} %concatenate.43), channel_id=1, source_target_pairs={{0,14},{2,0},{4,2},{6,4},{8,6},{10,8},{12,10},{14,12},{1,15},{3,1}... | collective-permute-start | bytes 1048328 | tf_op jit(solution)/shard_map/ppermute | solution.py:33
  21.9 3.9 %collective-permute-done.3 = bf16[520,336]{1,0:T(8,128)(2,1)S(1)} collective-permute-done((bf16[520,336]{1,0:T(8,128)(2,1)S(1)}, bf16[520,336]{1,0:T(8,128)(2,1)S(1)}, u32[]{:S(2)}, u32[]{:S(2)}) %collective-permute-start.3) | collective-permute-done | bytes 349472 | tf_op jit(solution)/shard_map/ppermute | solution.py:30
  25.8 2.8 %collective-permute-start.4 = (bf16[520,336]{1,0:T(8,128)(2,1)S(1)}, bf16[520,336]{1,0:T(8,128)(2,1)S(1)}, u32[]{:S(2)}, u32[]{:S(2)}) collective-permute-start(bf16[520,336]{1,0:T(8,128)(2,1)S(1)} %collective-permute-done.3), channel_id=1, source_target_pairs={{0,2},{2,4},{4,6},{6,8},{8,10},{10,12},{12,14},{14,0},{1,3},{3,5},... | collective-permute-start | bytes 1048328 | tf_op jit(solution)/shard_map/ppermute | solution.py:30
  28.6 4.2 %collective-permute-start.1 = (bf16[520,336]{1,0:T(8,128)(2,1)S(1)}, bf16[520,336]{1,0:T(8,128)(2,1)S(1)}, u32[]{:S(2)}, u32[]{:S(2)}) collective-permute-start(bf16[520,336]{1,0:T(8,128)(2,1)S(1)} %collective-permute-done), channel_id=1, source_target_pairs={{0,14},{2,0},{4,2},{6,4},{8,6},{10,8},{12,10},{14,12},{1,15},{3,1}... | collective-permute-start | bytes 1048328 | tf_op jit(solution)/shard_map/ppermute | solution.py:33
  32.8 3.9 %collective-permute-done.4 = bf16[520,336]{1,0:T(8,128)(2,1)S(1)} collective-permute-done((bf16[520,336]{1,0:T(8,128)(2,1)S(1)}, bf16[520,336]{1,0:T(8,128)(2,1)S(1)}, u32[]{:S(2)}, u32[]{:S(2)}) %collective-permute-start.4) | collective-permute-done | bytes 349472 | tf_op jit(solution)/shard_map/ppermute | solution.py:30
  36.7 3.9 %collective-permute-start.5 = (bf16[520,336]{1,0:T(8,128)(2,1)S(1)}, bf16[520,336]{1,0:T(8,128)(2,1)S(1)}, u32[]{:S(2)}, u32[]{:S(2)}) collective-permute-start(bf16[520,336]{1,0:T(8,128)(2,1)S(1)} %collective-permute-done.4), channel_id=1, source_target_pairs={{0,2},{2,4},{4,6},{6,8},{8,10},{10,12},{12,14},{14,0},{1,3},{3,5},... | collective-permute-start | bytes 1048328 | tf_op jit(solution)/shard_map/ppermute | solution.py:30
  41.2 2.6 %collective-permute-start.2 = (bf16[520,336]{1,0:T(8,128)(2,1)S(1)}, bf16[520,336]{1,0:T(8,128)(2,1)S(1)}, u32[]{:S(2)}, u32[]{:S(2)}) collective-permute-start(bf16[520,336]{1,0:T(8,128)(2,1)S(1)} %collective-permute-done.1), channel_id=1, source_target_pairs={{0,14},{2,0},{4,2},{6,4},{8,6},{10,8},{12,10},{14,12},{1,15},{3,1}... | collective-permute-start | bytes 1048328 | tf_op jit(solution)/shard_map/ppermute | solution.py:33
  43.8 3.9 %collective-permute-done.5 = bf16[520,336]{1,0:T(8,128)(2,1)S(1)} collective-permute-done((bf16[520,336]{1,0:T(8,128)(2,1)S(1)}, bf16[520,336]{1,0:T(8,128)(2,1)S(1)}, u32[]{:S(2)}, u32[]{:S(2)}) %collective-permute-start.5) | collective-permute-done | bytes 349472 | tf_op jit(solution)/shard_map/ppermute | solution.py:30
  47.6 4.6 %collective-permute-start.6 = (bf16[520,336]{1,0:T(8,128)(2,1)S(1)}, bf16[520,336]{1,0:T(8,128)(2,1)S(1)}, u32[]{:S(2)}, u32[]{:S(2)}) collective-permute-start(bf16[520,336]{1,0:T(8,128)(2,1)S(1)} %collective-permute-done.5), channel_id=1, source_target_pairs={{0,2},{2,4},{4,6},{6,8},{8,10},{10,12},{12,14},{14,0},{1,3},{3,5},... | collective-permute-start | bytes 1048328 | tf_op jit(solution)/shard_map/ppermute | solution.py:30
  53.6 5.0 %collective-permute-done.6 = bf16[520,336]{1,0:T(8,128)(2,1)S(1)} collective-permute-done((bf16[520,336]{1,0:T(8,128)(2,1)S(1)}, bf16[520,336]{1,0:T(8,128)(2,1)S(1)}, u32[]{:S(2)}, u32[]{:S(2)}) %collective-permute-start.6) | collective-permute-done | bytes 349472 | tf_op jit(solution)/shard_map/ppermute | solution.py:30
  58.6 7.6 %concatenate.44 = bf16[520,5376]{1,0:T(8,128)(2,1)} concatenate(bf16[520,336]{1,0:T(8,128)(2,1)S(1)} %concatenate.43, bf16[520,336]{1,0:T(8,128)(2,1)S(1)} %collective-permute-done, bf16[520,336]{1,0:T(8,128)(2,1)S(1)} %collective-permute-done.1, bf16[520,336]{1,0:T(8,128)(2,1)S(1)} %collective-permute-done.2, bf16[520,336]{1,0:T(8,128)(2,1)S(1)} %collective-permute-done.6, ...), dimensions={1} | concatenate | bytes 11182080 | tf_op jit(solution)/shard_map/concatenate | solution.py:39
  66.2 3.3 %constant_dynamic-slice_fusion = bf16[520,2688]{1,0:T(8,128)(2,1)S(1)} fusion(bf16[520,5376]{1,0:T(8,128)(2,1)} %concatenate.44, s32[]{:T(128)S(6)} %select_n.22), kind=kLoop, calls=%fused_computation.80 | loop fusion | bytes 5591044 | tf_op jit(solution)/shard_map/dynamic_slice | solution.py:41
  69.5 2.1 %collective-permute-start.7 = (bf16[520,2688]{1,0:T(8,128)(2,1)S(1)}, bf16[520,2688]{1,0:T(8,128)(2,1)}, u32[]{:S(2)}, u32[]{:S(2)}) collective-permute-start(bf16[520,2688]{1,0:T(8,128)(2,1)S(1)} %constant_dynamic-slice_fusion), channel_id=1, source_target_pairs={{0,1},{1,0},{2,3},{3,2},{4,5},{5,4},{6,7},{7,6},{8,9},{9,8},{10,11... | collective-permute-start | bytes 8386568 | tf_op jit(solution)/shard_map/ppermute | solution.py:30
  76.7 5.2 %fusion.5 = bf16[520,5376]{1,0:T(8,128)(2,1)S(1)} fusion(s32[]{:T(128)S(6)} %select_n.24, bf16[520,2688]{1,0:T(8,128)(2,1)S(1)} %constant_dynamic-slice_fusion, bf16[520,2688]{1,0:T(8,128)(2,1)} %collective-permute-done.7), kind=kLoop, calls=%fused_computation.13 | loop fusion | flops 22364160 | bytes 11182084 | tf_op jit(solution)/shard_map/concatenate | solution.py:39
  82.0 2.4 %copy-done = bf16[520,5376]{1,0:T(8,128)(2,1)} copy-done((bf16[520,5376]{1,0:T(8,128)(2,1)}, bf16[520,5376]{1,0:T(8,128)(2,1)S(1)}, u32[]{:S(2)}) %copy-start) | copy-done | bytes 5591064
  85.5 22.3 %all-gather.2.cloned.1.call-done = bf16[5632,512]{1,0:T(8,128)(2,1)} async-done(((bf16[176,512]{1,0:T(8,128)(2,1)}), bf16[5632,512]{1,0:T(8,128)(2,1)}) %all-gather.2.cloned.1.call-update) | async-done | bytes 5767184 | tf_op jit(solution)/shard_map/all_gather | solution.py:87
  108.9 3.2 %fusion.47 = (bf16[32,168,256]{2,1,0:T(8,128)(2,1)S(1)}, bf16[32,168,256]{2,1,0:T(8,128)(2,1)S(1)}) fusion(bf16[32,176,512]{2,1,0:T(8,128)(2,1)} %bitcast.66), kind=kLoop, calls=%fused_computation.90 | loop fusion | bytes 11010048 | tf_op jit(solution)/shard_map/slice | solution.py:91
  113.6 2.0 %fusion.23 = f32[512,256]{0,1:T(8,128)S(1)} fusion(bf16[5376,256]{1,0:T(8,128)(2,1)S(1)} %bitcast.68, f32[5376]{0:T(1024)S(1)} %fusion.39, f32[512]{0:T(512)S(1)} %add_rsqrt_fusion.2, bf16[520,5376]{1,0:T(8,128)(2,1)S(1)} %bitcast.61), kind=kOutput, calls=%fused_computation.32 | convolution fusion | flops 1420296192 | bytes 8808448 | tf_op jit(solution)/shard_map/dot_general | solution.py:120
  116.4 4.1 %collective-permute-start.8 = (bf16[512,2,128]{0,2,1:T(8,128)(2,1)S(1)}, bf16[512,2,128]{0,2,1:T(8,128)(2,1)}, u32[]{:S(2)}, u32[]{:S(2)}) collective-permute-start(bf16[512,2,128]{0,2,1:T(8,128)(2,1)S(1)} %pad_maximum_fusion), channel_id=1, source_target_pairs={{0,32},{16,48},{32,64},{48,80},{64,96},{80,112},{96,128},{112,144}... | collective-permute-start | bytes 786440 | tf_op jit(solution)/shard_map/ppermute | solution.py:19
  120.4 2.9 %collective-permute-start.9 = (bf16[512,2,128]{0,2,1:T(8,128)(2,1)S(1)}, bf16[512,2,128]{0,2,1:T(8,128)(2,1)}, u32[]{:S(2)}, u32[]{:S(2)}) collective-permute-start(bf16[512,2,128]{0,2,1:T(8,128)(2,1)S(1)} %pad_maximum_fusion), channel_id=1, source_target_pairs={{0,16},{16,32},{32,48},{48,64},{64,80},{80,96},{96,112},{112,128},... | collective-permute-start | bytes 786440 | tf_op jit(solution)/shard_map/ppermute | solution.py:19
  123.5 3.0 %copy.46 = bf16[256,5376]{1,0:T(8,128)(2,1)} copy(bf16[256,5376]{0,1:T(8,128)(2,1)S(1)} %bitcast.64) | data formatting | bytes 5505024 | tf_op jit(solution)/shard_map/dot_general | solution.py:123
  126.5 5.2 %multiply_reduce_fusion = (f32[512,2]{0,1:T(2,128)S(1)}, f32[512,2,128]{0,2,1:T(8,128)S(1)}) fusion(bf16[2,128,5376]{2,1,0:T(8,128)(2,1)} %bitcast.67, f32[5376]{0:T(1024)} %copy-done.2, f32[512]{0:T(512)S(1)} %add_rsqrt_fusion.2, bf16[520,5376]{1,0:T(8,128)(2,1)} %copy-done), kind=kOutput, calls=%fused_computation.35 | convolution fusion | flops 1420557312 | bytes 8812544 | tf_op jit(solution)/shard_map/dot_general | solution.py:123
  134.8 2.0 %fusion.19 = bf16[128,2,512]{2,0,1:T(8,128)(2,1)S(1)} fusion(f32[2,512]{1,0:T(2,128)S(1)} %get-tuple-element.22, f32[1536,512,2]{1,0,2:T(8,128)S(1)} %get-tuple-element.23, pred[512,1536]{0,1:T(8,128)(4,1)S(1)} %copy-done.1, bf16[1536,2,128]{0,2,1:T(8,128)(2,1)S(1)} %maximum_maximum_fusion), kind=kOutput, calls=%fused_computation.31 | convolution fusion | flops 409075712 | bytes 7737344 | tf_op jit(solution)/shard_map/kgts,skd->tkgd/dot_general | solution.py:153
  (67 shorter events, 20.5 us)
Async XLA Ops:
  6.5 101.3 %all-gather.2.cloned.1.call-start = ((), (), s32[]{:S(2)}) async-start(), calls=%async_computation | async-start | bytes 5947392 | tf_op jit(solution)/shard_map/all_gather | solution.py:87
  12.2 13.5 %collective-permute-start.3 = (bf16[520,336]{1,0:T(8,128)(2,1)S(1)}, bf16[520,336]{1,0:T(8,128)(2,1)S(1)}, u32[]{:S(2)}, u32[]{:S(2)}) collective-permute-start(bf16[520,336]{1,0:T(8,128)(2,1)S(1)} %concatenate.43), channel_id=1, source_target_pairs={{0,2},{2,4},{4,6},{6,8},{8,10},{10,12},{12,14},{14,0},{1,3},{3,5},... | collective-permute-start | bytes 1048328 | tf_op jit(solution)/shard_map/ppermute | solution.py:30
  15.7 12.9 %collective-permute-start = (bf16[520,336]{1,0:T(8,128)(2,1)S(1)}, bf16[520,336]{1,0:T(8,128)(2,1)S(1)}, u32[]{:S(2)}, u32[]{:S(2)}) collective-permute-start(bf16[520,336]{1,0:T(8,128)(2,1)S(1)} %concatenate.43), channel_id=1, source_target_pairs={{0,14},{2,0},{4,2},{6,4},{8,6},{10,8},{12,10},{14,12},{1,15},{3,1}... | collective-permute-start | bytes 1048328 | tf_op jit(solution)/shard_map/ppermute | solution.py:33
  25.8 10.9 %collective-permute-start.4 = (bf16[520,336]{1,0:T(8,128)(2,1)S(1)}, bf16[520,336]{1,0:T(8,128)(2,1)S(1)}, u32[]{:S(2)}, u32[]{:S(2)}) collective-permute-start(bf16[520,336]{1,0:T(8,128)(2,1)S(1)} %collective-permute-done.3), channel_id=1, source_target_pairs={{0,2},{2,4},{4,6},{6,8},{8,10},{10,12},{12,14},{14,0},{1,3},{3,5},... | collective-permute-start | bytes 1048328 | tf_op jit(solution)/shard_map/ppermute | solution.py:30
  28.6 12.6 %collective-permute-start.1 = (bf16[520,336]{1,0:T(8,128)(2,1)S(1)}, bf16[520,336]{1,0:T(8,128)(2,1)S(1)}, u32[]{:S(2)}, u32[]{:S(2)}) collective-permute-start(bf16[520,336]{1,0:T(8,128)(2,1)S(1)} %collective-permute-done), channel_id=1, source_target_pairs={{0,14},{2,0},{4,2},{6,4},{8,6},{10,8},{12,10},{14,12},{1,15},{3,1}... | collective-permute-start | bytes 1048328 | tf_op jit(solution)/shard_map/ppermute | solution.py:33
  36.7 10.9 %collective-permute-start.5 = (bf16[520,336]{1,0:T(8,128)(2,1)S(1)}, bf16[520,336]{1,0:T(8,128)(2,1)S(1)}, u32[]{:S(2)}, u32[]{:S(2)}) collective-permute-start(bf16[520,336]{1,0:T(8,128)(2,1)S(1)} %collective-permute-done.4), channel_id=1, source_target_pairs={{0,2},{2,4},{4,6},{6,8},{8,10},{10,12},{12,14},{14,0},{1,3},{3,5},... | collective-permute-start | bytes 1048328 | tf_op jit(solution)/shard_map/ppermute | solution.py:30
  41.2 12.4 %collective-permute-start.2 = (bf16[520,336]{1,0:T(8,128)(2,1)S(1)}, bf16[520,336]{1,0:T(8,128)(2,1)S(1)}, u32[]{:S(2)}, u32[]{:S(2)}) collective-permute-start(bf16[520,336]{1,0:T(8,128)(2,1)S(1)} %collective-permute-done.1), channel_id=1, source_target_pairs={{0,14},{2,0},{4,2},{6,4},{8,6},{10,8},{12,10},{14,12},{1,15},{3,1}... | collective-permute-start | bytes 1048328 | tf_op jit(solution)/shard_map/ppermute | solution.py:33
  47.6 10.9 %collective-permute-start.6 = (bf16[520,336]{1,0:T(8,128)(2,1)S(1)}, bf16[520,336]{1,0:T(8,128)(2,1)S(1)}, u32[]{:S(2)}, u32[]{:S(2)}) collective-permute-start(bf16[520,336]{1,0:T(8,128)(2,1)S(1)} %collective-permute-done.5), channel_id=1, source_target_pairs={{0,2},{2,4},{4,6},{6,8},{8,10},{10,12},{12,14},{14,0},{1,3},{3,5},... | collective-permute-start | bytes 1048328 | tf_op jit(solution)/shard_map/ppermute | solution.py:30
  69.5 7.2 %collective-permute-start.7 = (bf16[520,2688]{1,0:T(8,128)(2,1)S(1)}, bf16[520,2688]{1,0:T(8,128)(2,1)}, u32[]{:S(2)}, u32[]{:S(2)}) collective-permute-start(bf16[520,2688]{1,0:T(8,128)(2,1)S(1)} %constant_dynamic-slice_fusion), channel_id=1, source_target_pairs={{0,1},{1,0},{2,3},{3,2},{4,5},{5,4},{6,7},{7,6},{8,9},{9,8},{10,11... | collective-permute-start | bytes 8386568 | tf_op jit(solution)/shard_map/ppermute | solution.py:30
  81.8 2.5 %copy-start = (bf16[520,5376]{1,0:T(8,128)(2,1)}, bf16[520,5376]{1,0:T(8,128)(2,1)S(1)}, u32[]{:S(2)}) copy-start(bf16[520,5376]{1,0:T(8,128)(2,1)S(1)} %fusion.5) | copy-start | bytes 16773124
  84.3 29.2 %copy-start.2 = (f32[5376]{0:T(1024)}, f32[5376]{0:T(1024)S(1)}, u32[]{:S(2)}) copy-start(f32[5376]{0:T(1024)S(1)} %fusion.39) | copy-start | bytes 64516
  108.9 4.7 %slice-start = ((s8[5591040]{0:T(1024)(128)(4,1)}), s8[4194304]{0:T(1024)(128)(4,1)S(1)}, s32[]{:S(2)}) async-start(s8[5591040]{0:T(1024)(128)(4,1)} %bitcast.60), calls=%async_computation.1 | async-start | bytes 8388608
  112.1 1.5 %slice-start.1 = ((s8[5591040]{0:T(1024)(128)(4,1)}), s8[1396736]{0:T(1024)(128)(4,1)S(1)}, s32[]{:S(2)}) async-start(s8[5591040]{0:T(1024)(128)(4,1)} %bitcast.60), calls=%async_computation.2 | async-start | bytes 2793472
  113.6 2.1 %copy-start.3 = (f32[128]{0:T(128)S(1)}, f32[128]{0:T(128)}, u32[]{:S(2)}) copy-start(f32[128]{0:T(128)} %param.10) | copy-start | bytes 1540
  116.4 15.6 %collective-permute-start.8 = (bf16[512,2,128]{0,2,1:T(8,128)(2,1)S(1)}, bf16[512,2,128]{0,2,1:T(8,128)(2,1)}, u32[]{:S(2)}, u32[]{:S(2)}) collective-permute-start(bf16[512,2,128]{0,2,1:T(8,128)(2,1)S(1)} %pad_maximum_fusion), channel_id=1, source_target_pairs={{0,32},{16,48},{32,64},{48,80},{64,96},{80,112},{96,128},{112,144}... | collective-permute-start | bytes 786440 | tf_op jit(solution)/shard_map/ppermute | solution.py:19
  120.4 11.5 %collective-permute-start.9 = (bf16[512,2,128]{0,2,1:T(8,128)(2,1)S(1)}, bf16[512,2,128]{0,2,1:T(8,128)(2,1)}, u32[]{:S(2)}, u32[]{:S(2)}) collective-permute-start(bf16[512,2,128]{0,2,1:T(8,128)(2,1)S(1)} %pad_maximum_fusion), channel_id=1, source_target_pairs={{0,16},{16,32},{32,48},{48,64},{64,80},{80,96},{96,112},{112,128},... | collective-permute-start | bytes 786440 | tf_op jit(solution)/shard_map/ppermute | solution.py:19
  126.5 5.2 %copy-start.4 = (f32[128]{0:T(128)S(1)}, f32[128]{0:T(128)}, u32[]{:S(2)}) copy-start(f32[128]{0:T(128)} %param.9) | copy-start | bytes 1540
  126.5 6.5 %copy-start.1 = (pred[512,1536]{0,1:T(8,128)(4,1)S(1)}, pred[512,1536]{0,1:T(8,128)(4,1)}, u32[]{:S(2)}) copy-start(pred[512,1536]{0,1:T(8,128)(4,1)} %fusion.16) | copy-start | bytes 2359300
Sparse Core Ops, SparseCore 0:
  10.5 97.2 all-gather.1
where the time goes:
time: 145 us; the launch traced here: 144 us
  waiting for transfers between devices  42.1 us (29%)
  starting transfers between devices  36.8 us (25%)
  local copies, waits for them, and re-layouts  25.3 us (17%)
  other arithmetic  14.9 us (10%)
  between operations  14.5 us (10%)
  matrix products  10.9 us (8%)
    all_gather x1, waiting for transfers between devices, local(): lax.all_gather(padded, ROW, axis=0, tiled=True)  22.3 us
    ppermute x5, waiting for transfers between devices, ring_gather(): forward = lax.ppermute(forward, axis, right)  17.8 us
    ppermute x5, starting transfers between devices, ring_gather(): forward = lax.ppermute(forward, axis, right)  16.9 us
    ppermute x3, starting transfers between devices, ring_gather(): backward = lax.ppermute(backward, axis, left)  13 us
    concatenate x1, local copies, waits for them, and re-layouts, ring_gather(): doubled = jnp.concatenate([stacked, stacked], axis=dim)  7.61 us
    ppermute x2, starting transfers between devices, shifted(): return lax.ppermute(array, axis, pairs)  6.96 us
    unnamed x17, local copies, waits for them, and re-layouts  5.32 us
    dot_general x1, matrix products, local(): jnp.dot(whole, ordered(0, query_cols), preferred_element_type=jnp.float32)  5.2 us
  transfers between devices with their start and end apart: 11, of which 8 were waited for; matrix products, arithmetic and copies ran while one was open for 22% of the time, Pallas kernels for 0%

commit v1 on v0

--- a/solution.py
+++ b/solution.py
@@ -11,6 +11,15 @@
 QUERY_SCALAR = 168.0
 ROPE_BASE = 10000.0
 ROW = ("rz", "rx")
+
+
+def set_terms(target):
+    return jnp.concatenate(
+        jax.lax.all_to_all(
+            jnp.stack([target] * jax.lax.axis_size(ROW)), axis_name=ROW, split_axis=0, concat_axis=0
+        ),
+        axis=0,
+    )
 
 
 def shifted(array, axis, by):
@@ -84,7 +93,7 @@
         ],
         axis=0,
     )
-    slabs = lax.all_gather(padded, ROW, axis=0, tiled=True).reshape(-1, aligned, weight_cols)
+    slabs = set_terms(padded).reshape(-1, aligned, weight_cols)
     largest = jnp.max(slabs[:, weight_rows].astype(jnp.float32), axis=0)
 
     def clipped_columns(first, last):

time: 145 us -> 184 us (1.27)
  the two profiles are of different devices: /device:TPU:8 before, /device:TPU:1 now
where the time goes in v1:
time: 184 us; the launch traced here: 183 us
  waiting for transfers between devices  74.6 us (41%)
  starting transfers between devices  55.6 us (30%)
  local copies, waits for them, and re-layouts  27.3 us (15%)
  other arithmetic  13.4 us (7%)
  matrix products  10.9 us (6%)
    all_to_all x1, waiting for transfers between devices, set_terms(): jax.lax.all_to_all(jnp.stack([target] * jax.lax.axis_size(ROW)), axis_nam...  46.8 us
    ppermute x5, waiting for transfers between devices, ring_gather(): forward = lax.ppermute(forward, axis, right)  27.8 us
    ppermute x5, starting transfers between devices, ring_gather(): forward = lax.ppermute(forward, axis, right)  14.9 us
    all_to_all x1, starting transfers between devices, set_terms(): jax.lax.all_to_all(jnp.stack([target] * jax.lax.axis_size(ROW)), axis_nam...  14 us
    ppermute x2, starting transfers between devices, shifted(): return lax.ppermute(array, axis, pairs)  13.7 us
    ppermute x3, starting transfers between devices, ring_gather(): backward = lax.ppermute(backward, axis, left)  13 us
    concatenate x1, local copies, waits for them, and re-layouts, ring_gather(): doubled = jnp.concatenate([stacked, stacked], axis=dim)  7.59 us
    dot_general x1, matrix products, local(): jnp.dot(whole, ordered(0, query_cols), preferred_element_type=jnp.float32)  5.2 us
  transfers between devices with their start and end apart: 11, of which 6 were waited for; matrix products, arithmetic and copies ran while one was open for 16% of the time, Pallas kernels for 0%

profile of v1, /device:TPU:1, one launch (start us, length us, event | category | flops | bytes accessed | tf_op | source)
XLA Modules:
  0.0 182.9 jit_solution(8257374237342944789)
XLA Ops:
  2.7 3.1 %stack.2 = bf16[32,176,512]{2,1,0:T(8,128)(2,1)} broadcast(bf16[176,512]{1,0:T(8,128)(2,1)S(1)} %maximum_maximum_fusion.1), dimensions={1,2} | broadcast | bytes 5947392 | tf_op jit(solution)/shard_map/stack | solution.py:19
  5.9 14.0 %all-to-all-start = ((bf16[32,176,512]{2,1,0:T(8,128)(2,1)}), bf16[32,176,512]{2,1,0:T(8,128)(2,1)}, u32[]{:S(2)}, u32[]{:S(2)}) async-start(bf16[32,176,512]{2,1,0:T(8,128)(2,1)} %stack.2), calls=%async_computation | async-start | bytes 11534336 | tf_op jit(solution)/shard_map/all_to_all | solution.py:18
  20.4 3.2 %collective-permute-start.3 = (bf16[520,336]{1,0:T(8,128)(2,1)S(1)}, bf16[520,336]{1,0:T(8,128)(2,1)S(1)}, u32[]{:S(2)}, u32[]{:S(2)}) collective-permute-start(bf16[520,336]{1,0:T(8,128)(2,1)S(1)} %concatenate.43), channel_id=1, source_target_pairs={{0,2},{2,4},{4,6},{6,8},{8,10},{10,12},{12,14},{14,0},{1,3},{3,5},... | collective-permute-start | bytes 1048328 | tf_op jit(solution)/shard_map/ppermute | solution.py:39
  23.6 3.8 %collective-permute-start = (bf16[520,336]{1,0:T(8,128)(2,1)S(1)}, bf16[520,336]{1,0:T(8,128)(2,1)S(1)}, u32[]{:S(2)}, u32[]{:S(2)}) collective-permute-start(bf16[520,336]{1,0:T(8,128)(2,1)S(1)} %concatenate.43), channel_id=1, source_target_pairs={{0,14},{2,0},{4,2},{6,4},{8,6},{10,8},{12,10},{14,12},{1,15},{3,1}... | collective-permute-start | bytes 1048328 | tf_op jit(solution)/shard_map/ppermute | solution.py:42
  27.4 6.8 %collective-permute-done.3 = bf16[520,336]{1,0:T(8,128)(2,1)S(1)} collective-permute-done((bf16[520,336]{1,0:T(8,128)(2,1)S(1)}, bf16[520,336]{1,0:T(8,128)(2,1)S(1)}, u32[]{:S(2)}, u32[]{:S(2)}) %collective-permute-start.3) | collective-permute-done | bytes 349472 | tf_op jit(solution)/shard_map/ppermute | solution.py:39
  36.2 4.6 %collective-permute-start.1 = (bf16[520,336]{1,0:T(8,128)(2,1)S(1)}, bf16[520,336]{1,0:T(8,128)(2,1)S(1)}, u32[]{:S(2)}, u32[]{:S(2)}) collective-permute-start(bf16[520,336]{1,0:T(8,128)(2,1)S(1)} %collective-permute-done), channel_id=1, source_target_pairs={{0,14},{2,0},{4,2},{6,4},{8,6},{10,8},{12,10},{14,12},{1,15},{3,1}... | collective-permute-start | bytes 1048328 | tf_op jit(solution)/shard_map/ppermute | solution.py:42
  40.7 6.0 %collective-permute-done.4 = bf16[520,336]{1,0:T(8,128)(2,1)S(1)} collective-permute-done((bf16[520,336]{1,0:T(8,128)(2,1)S(1)}, bf16[520,336]{1,0:T(8,128)(2,1)S(1)}, u32[]{:S(2)}, u32[]{:S(2)}) %collective-permute-start.4) | collective-permute-done | bytes 349472 | tf_op jit(solution)/shard_map/ppermute | solution.py:39
  48.6 4.6 %collective-permute-start.2 = (bf16[520,336]{1,0:T(8,128)(2,1)S(1)}, bf16[520,336]{1,0:T(8,128)(2,1)S(1)}, u32[]{:S(2)}, u32[]{:S(2)}) collective-permute-start(bf16[520,336]{1,0:T(8,128)(2,1)S(1)} %collective-permute-done.1), channel_id=1, source_target_pairs={{0,14},{2,0},{4,2},{6,4},{8,6},{10,8},{12,10},{14,12},{1,15},{3,1}... | collective-permute-start | bytes 1048328 | tf_op jit(solution)/shard_map/ppermute | solution.py:42
  53.2 5.2 %collective-permute-done.5 = bf16[520,336]{1,0:T(8,128)(2,1)S(1)} collective-permute-done((bf16[520,336]{1,0:T(8,128)(2,1)S(1)}, bf16[520,336]{1,0:T(8,128)(2,1)S(1)}, u32[]{:S(2)}, u32[]{:S(2)}) %collective-permute-start.5) | collective-permute-done | bytes 349472 | tf_op jit(solution)/shard_map/ppermute | solution.py:39
  60.3 8.9 %collective-permute-done.6 = bf16[520,336]{1,0:T(8,128)(2,1)S(1)} collective-permute-done((bf16[520,336]{1,0:T(8,128)(2,1)S(1)}, bf16[520,336]{1,0:T(8,128)(2,1)S(1)}, u32[]{:S(2)}, u32[]{:S(2)}) %collective-permute-start.6) | collective-permute-done | bytes 349472 | tf_op jit(solution)/shard_map/ppermute | solution.py:39
  69.3 7.6 %concatenate.44 = bf16[520,5376]{1,0:T(8,128)(2,1)} concatenate(bf16[520,336]{1,0:T(8,128)(2,1)S(1)} %concatenate.43, bf16[520,336]{1,0:T(8,128)(2,1)S(1)} %collective-permute-done, bf16[520,336]{1,0:T(8,128)(2,1)S(1)} %collective-permute-done.1, bf16[520,336]{1,0:T(8,128)(2,1)S(1)} %collective-permute-done.2, bf16[520,336]{1,0:T(8,128)(2,1)S(1)} %collective-permute-done.6, ...), dimensions={1} | concatenate | bytes 11182080 | tf_op jit(solution)/shard_map/concatenate | solution.py:48
  76.8 3.3 %constant_dynamic-slice_fusion = bf16[520,2688]{1,0:T(8,128)(2,1)S(1)} fusion(bf16[520,5376]{1,0:T(8,128)(2,1)} %concatenate.44, s32[]{:T(128)S(6)} %select_n.22), kind=kLoop, calls=%fused_computation.80 | loop fusion | bytes 5591044 | tf_op jit(solution)/shard_map/dynamic_slice | solution.py:50
  80.1 6.0 %collective-permute-start.7 = (bf16[520,2688]{1,0:T(8,128)(2,1)S(1)}, bf16[520,2688]{1,0:T(8,128)(2,1)}, u32[]{:S(2)}, u32[]{:S(2)}) collective-permute-start(bf16[520,2688]{1,0:T(8,128)(2,1)S(1)} %constant_dynamic-slice_fusion), channel_id=1, source_target_pairs={{0,1},{1,0},{2,3},{3,2},{4,5},{5,4},{6,7},{7,6},{8,9},{9,8},{10,11... | collective-permute-start | bytes 8386568 | tf_op jit(solution)/shard_map/ppermute | solution.py:39
  87.9 2.0 %fusion.16 = pred[512,1536]{0,1:T(8,128)(4,1)} fusion(s32[1536]{0:T(1024)S(1)} %iota_add_fusion, s32[512]{0:T(512)S(1)} %iota_add_fusion.1, pred[1536]{0:T(1024)(128)(4,1)S(1)} %broadcast_compare_fusion), kind=kLoop, calls=%fused_computation.28 | loop fusion | flops 3932160 | bytes 796160 | tf_op jit(solution)/shard_map/and | solution.py:158
  90.8 5.2 %fusion.5 = bf16[520,5376]{1,0:T(8,128)(2,1)S(1)} fusion(s32[]{:T(128)S(6)} %select_n.24, bf16[520,2688]{1,0:T(8,128)(2,1)S(1)} %constant_dynamic-slice_fusion, bf16[520,2688]{1,0:T(8,128)(2,1)} %collective-permute-done.7), kind=kLoop, calls=%fused_computation.13 | loop fusion | flops 22364160 | bytes 11182084 | tf_op jit(solution)/shard_map/concatenate | solution.py:48
  96.1 2.3 %copy-done = bf16[520,5376]{1,0:T(8,128)(2,1)} copy-done((bf16[520,5376]{1,0:T(8,128)(2,1)}, bf16[520,5376]{1,0:T(8,128)(2,1)S(1)}, u32[]{:S(2)}) %copy-start) | copy-done | bytes 5591064
  99.6 46.8 %all-to-all-done = bf16[32,176,512]{2,1,0:T(8,128)(2,1)} async-done(((bf16[32,176,512]{2,1,0:T(8,128)(2,1)}), bf16[32,176,512]{2,1,0:T(8,128)(2,1)}, u32[]{:S(2)}, u32[]{:S(2)}) %all-to-all-start) | async-done | bytes 5767200 | tf_op jit(solution)/shard_map/all_to_all | solution.py:18
  147.4 3.2 %fusion.47 = (bf16[32,168,256]{2,1,0:T(8,128)(2,1)S(1)}, bf16[32,168,256]{2,1,0:T(8,128)(2,1)S(1)}) fusion(bf16[32,176,512]{2,1,0:T(8,128)(2,1)} %all-to-all-done), kind=kLoop, calls=%fused_computation.90 | loop fusion | bytes 11010048 | tf_op jit(solution)/shard_map/slice | solution.py:100
  152.1 2.0 %fusion.23 = f32[512,256]{0,1:T(8,128)S(1)} fusion(bf16[5376,256]{1,0:T(8,128)(2,1)S(1)} %bitcast.65, f32[5376]{0:T(1024)S(1)} %fusion.39, f32[512]{0:T(512)S(1)} %add_rsqrt_fusion.2, bf16[520,5376]{1,0:T(8,128)(2,1)S(1)} %bitcast.60), kind=kOutput, calls=%fused_computation.32 | convolution fusion | flops 1420296192 | bytes 8808448 | tf_op jit(solution)/shard_map/dot_general | solution.py:129
  154.9 7.1 %collective-permute-start.8 = (bf16[512,2,128]{0,2,1:T(8,128)(2,1)S(1)}, bf16[512,2,128]{0,2,1:T(8,128)(2,1)}, u32[]{:S(2)}, u32[]{:S(2)}) collective-permute-start(bf16[512,2,128]{0,2,1:T(8,128)(2,1)S(1)} %pad_maximum_fusion), channel_id=1, source_target_pairs={{0,32},{16,48},{32,64},{48,80},{64,96},{80,112},{96,128},{112,144}... | collective-permute-start | bytes 786440 | tf_op jit(solution)/shard_map/ppermute | solution.py:28
  161.9 6.7 %collective-permute-start.9 = (bf16[512,2,128]{0,2,1:T(8,128)(2,1)S(1)}, bf16[512,2,128]{0,2,1:T(8,128)(2,1)}, u32[]{:S(2)}, u32[]{:S(2)}) collective-permute-start(bf16[512,2,128]{0,2,1:T(8,128)(2,1)S(1)} %pad_maximum_fusion), channel_id=1, source_target_pairs={{0,16},{16,32},{32,48},{48,64},{64,80},{80,96},{96,112},{112,128},... | collective-permute-start | bytes 786440 | tf_op jit(solution)/shard_map/ppermute | solution.py:28
  168.8 3.0 %copy.46 = bf16[256,5376]{1,0:T(8,128)(2,1)} copy(bf16[256,5376]{0,1:T(8,128)(2,1)S(1)} %bitcast.63) | data formatting | bytes 5505024 | tf_op jit(solution)/shard_map/dot_general | solution.py:132
  171.8 5.2 %multiply_reduce_fusion = (f32[512,2]{0,1:T(2,128)S(1)}, f32[512,2,128]{0,2,1:T(8,128)S(1)}) fusion(bf16[2,128,5376]{2,1,0:T(8,128)(2,1)} %bitcast.64, f32[5376]{0:T(1024)} %copy-done.3, f32[512]{0:T(512)S(1)} %add_rsqrt_fusion.2, bf16[520,5376]{1,0:T(8,128)(2,1)} %copy-done), kind=kOutput, calls=%fused_computation.35 | convolution fusion | flops 1420557312 | bytes 8812544 | tf_op jit(solution)/shard_map/dot_general | solution.py:132
  180.0 2.0 %fusion.19 = bf16[128,2,512]{2,0,1:T(8,128)(2,1)S(1)} fusion(f32[2,512]{1,0:T(2,128)S(1)} %get-tuple-element.22, f32[1536,512,2]{1,0,2:T(8,128)S(1)} %get-tuple-element.23, pred[512,1536]{0,1:T(8,128)(4,1)S(1)} %copy-done.1, bf16[1536,2,128]{0,2,1:T(8,128)(2,1)S(1)} %maximum_maximum_fusion), kind=kOutput, calls=%fused_computation.31 | convolution fusion | flops 409075712 | bytes 7737344 | tf_op jit(solution)/shard_map/kgts,skd->tkgd/dot_general | solution.py:162
  (71 shorter events, 19.5 us)
Async XLA Ops:
  5.8 14.0 %copy-start.4 = (f32[336]{0:T(512)S(1)}, f32[336]{0:T(512)}, u32[]{:S(2)}) copy-start(f32[336]{0:T(512)} %param.8) | copy-start | bytes 4036
  5.9 14.0 %copy-start.2 = (bf16[512,336]{0,1:T(8,128)(2,1)S(1)}, bf16[512,336]{0,1:T(8,128)(2,1)}, u32[]{:S(2)}) copy-start(bf16[512,336]{0,1:T(8,128)(2,1)} %param.7) | copy-start | bytes 1032196
  5.9 140.5 %all-to-all-start = ((bf16[32,176,512]{2,1,0:T(8,128)(2,1)}), bf16[32,176,512]{2,1,0:T(8,128)(2,1)}, u32[]{:S(2)}, u32[]{:S(2)}) async-start(bf16[32,176,512]{2,1,0:T(8,128)(2,1)} %stack.2), calls=%async_computation | async-start | bytes 11534336 | tf_op jit(solution)/shard_map/all_to_all | solution.py:18
  20.4 13.8 %collective-permute-start.3 = (bf16[520,336]{1,0:T(8,128)(2,1)S(1)}, bf16[520,336]{1,0:T(8,128)(2,1)S(1)}, u32[]{:S(2)}, u32[]{:S(2)}) collective-permute-start(bf16[520,336]{1,0:T(8,128)(2,1)S(1)} %concatenate.43), channel_id=1, source_target_pairs={{0,2},{2,4},{4,6},{6,8},{8,10},{10,12},{12,14},{14,0},{1,3},{3,5},... | collective-permute-start | bytes 1048328 | tf_op jit(solution)/shard_map/ppermute | solution.py:39
  23.6 12.6 %collective-permute-start = (bf16[520,336]{1,0:T(8,128)(2,1)S(1)}, bf16[520,336]{1,0:T(8,128)(2,1)S(1)}, u32[]{:S(2)}, u32[]{:S(2)}) collective-permute-start(bf16[520,336]{1,0:T(8,128)(2,1)S(1)} %concatenate.43), channel_id=1, source_target_pairs={{0,14},{2,0},{4,2},{6,4},{8,6},{10,8},{12,10},{14,12},{1,15},{3,1}... | collective-permute-start | bytes 1048328 | tf_op jit(solution)/shard_map/ppermute | solution.py:42
  34.2 12.5 %collective-permute-start.4 = (bf16[520,336]{1,0:T(8,128)(2,1)S(1)}, bf16[520,336]{1,0:T(8,128)(2,1)S(1)}, u32[]{:S(2)}, u32[]{:S(2)}) collective-permute-start(bf16[520,336]{1,0:T(8,128)(2,1)S(1)} %collective-permute-done.3), channel_id=1, source_target_pairs={{0,2},{2,4},{4,6},{6,8},{8,10},{10,12},{12,14},{14,0},{1,3},{3,5},... | collective-permute-start | bytes 1048328 | tf_op jit(solution)/shard_map/ppermute | solution.py:39
  36.2 12.5 %collective-permute-start.1 = (bf16[520,336]{1,0:T(8,128)(2,1)S(1)}, bf16[520,336]{1,0:T(8,128)(2,1)S(1)}, u32[]{:S(2)}, u32[]{:S(2)}) collective-permute-start(bf16[520,336]{1,0:T(8,128)(2,1)S(1)} %collective-permute-done), channel_id=1, source_target_pairs={{0,14},{2,0},{4,2},{6,4},{8,6},{10,8},{12,10},{14,12},{1,15},{3,1}... | collective-permute-start | bytes 1048328 | tf_op jit(solution)/shard_map/ppermute | solution.py:42
  46.7 11.7 %collective-permute-start.5 = (bf16[520,336]{1,0:T(8,128)(2,1)S(1)}, bf16[520,336]{1,0:T(8,128)(2,1)S(1)}, u32[]{:S(2)}, u32[]{:S(2)}) collective-permute-start(bf16[520,336]{1,0:T(8,128)(2,1)S(1)} %collective-permute-done.4), channel_id=1, source_target_pairs={{0,2},{2,4},{4,6},{6,8},{8,10},{10,12},{12,14},{14,0},{1,3},{3,5},... | collective-permute-start | bytes 1048328 | tf_op jit(solution)/shard_map/ppermute | solution.py:39
  48.6 11.7 %collective-permute-start.2 = (bf16[520,336]{1,0:T(8,128)(2,1)S(1)}, bf16[520,336]{1,0:T(8,128)(2,1)S(1)}, u32[]{:S(2)}, u32[]{:S(2)}) collective-permute-start(bf16[520,336]{1,0:T(8,128)(2,1)S(1)} %collective-permute-done.1), channel_id=1, source_target_pairs={{0,14},{2,0},{4,2},{6,4},{8,6},{10,8},{12,10},{14,12},{1,15},{3,1}... | collective-permute-start | bytes 1048328 | tf_op jit(solution)/shard_map/ppermute | solution.py:42
  58.4 10.9 %collective-permute-start.6 = (bf16[520,336]{1,0:T(8,128)(2,1)S(1)}, bf16[520,336]{1,0:T(8,128)(2,1)S(1)}, u32[]{:S(2)}, u32[]{:S(2)}) collective-permute-start(bf16[520,336]{1,0:T(8,128)(2,1)S(1)} %collective-permute-done.5), channel_id=1, source_target_pairs={{0,2},{2,4},{4,6},{6,8},{8,10},{10,12},{12,14},{14,0},{1,3},{3,5},... | collective-permute-start | bytes 1048328 | tf_op jit(solution)/shard_map/ppermute | solution.py:39
  80.1 10.7 %collective-permute-start.7 = (bf16[520,2688]{1,0:T(8,128)(2,1)S(1)}, bf16[520,2688]{1,0:T(8,128)(2,1)}, u32[]{:S(2)}, u32[]{:S(2)}) collective-permute-start(bf16[520,2688]{1,0:T(8,128)(2,1)S(1)} %constant_dynamic-slice_fusion), channel_id=1, source_target_pairs={{0,1},{1,0},{2,3},{3,2},{4,5},{5,4},{6,7},{7,6},{8,9},{9,8},{10,11... | collective-permute-start | bytes 8386568 | tf_op jit(solution)/shard_map/ppermute | solution.py:39
  96.0 2.4 %copy-start = (bf16[520,5376]{1,0:T(8,128)(2,1)}, bf16[520,5376]{1,0:T(8,128)(2,1)S(1)}, u32[]{:S(2)}) copy-start(bf16[520,5376]{1,0:T(8,128)(2,1)S(1)} %fusion.5) | copy-start | bytes 16773124
  98.4 53.6 %copy-start.3 = (f32[5376]{0:T(1024)}, f32[5376]{0:T(1024)S(1)}, u32[]{:S(2)}) copy-start(f32[5376]{0:T(1024)S(1)} %fusion.39) | copy-start | bytes 64516
  147.4 4.6 %slice-start = ((s8[5591040]{0:T(1024)(128)(4,1)}), s8[4194304]{0:T(1024)(128)(4,1)S(1)}, s32[]{:S(2)}) async-start(s8[5591040]{0:T(1024)(128)(4,1)} %bitcast.59), calls=%async_computation.1 | async-start | bytes 8388608
  150.5 1.5 slice-start.1
  152.1 2.1 %copy-start.5 = (f32[128]{0:T(128)S(1)}, f32[128]{0:T(128)}, u32[]{:S(2)}) copy-start(f32[128]{0:T(128)} %param.10) | copy-start | bytes 1540
  154.9 22.4 %collective-permute-start.8 = (bf16[512,2,128]{0,2,1:T(8,128)(2,1)S(1)}, bf16[512,2,128]{0,2,1:T(8,128)(2,1)}, u32[]{:S(2)}, u32[]{:S(2)}) collective-permute-start(bf16[512,2,128]{0,2,1:T(8,128)(2,1)S(1)} %pad_maximum_fusion), channel_id=1, source_target_pairs={{0,32},{16,48},{32,64},{48,80},{64,96},{80,112},{96,128},{112,144}... | collective-permute-start | bytes 786440 | tf_op jit(solution)/shard_map/ppermute | solution.py:28
  161.9 15.3 %collective-permute-start.9 = (bf16[512,2,128]{0,2,1:T(8,128)(2,1)S(1)}, bf16[512,2,128]{0,2,1:T(8,128)(2,1)}, u32[]{:S(2)}, u32[]{:S(2)}) collective-permute-start(bf16[512,2,128]{0,2,1:T(8,128)(2,1)S(1)} %pad_maximum_fusion), channel_id=1, source_target_pairs={{0,16},{16,32},{32,48},{48,64},{64,80},{80,96},{96,112},{112,128},... | collective-permute-start | bytes 786440 | tf_op jit(solution)/shard_map/ppermute | solution.py:28
  171.8 5.2 %copy-start.6 = (f32[128]{0:T(128)S(1)}, f32[128]{0:T(128)}, u32[]{:S(2)}) copy-start(f32[128]{0:T(128)} %param.9) | copy-start | bytes 1540
  171.8 6.5 %copy-start.1 = (pred[512,1536]{0,1:T(8,128)(4,1)S(1)}, pred[512,1536]{0,1:T(8,128)(4,1)}, u32[]{:S(2)}) copy-start(pred[512,1536]{0,1:T(8,128)(4,1)} %fusion.16) | copy-start | bytes 2359300
